TPU v7x, 512 devices: a whole 4x8x8 slice. The times are simulated.
512 devices in a mesh: fsdp: 16 (over y, core), expert: 32 (over x, z).
Axes of the slice: x: 4, y: 8, z: 8, core: 2. Of those that a mesh axis runs over, the one named last changes fastest.
Arguments:
- frames: bfloat16 [16, 4096, 1536], P('fsdp', 'expert'), may hold values from -6 to 6
- ln_gain: float32 [1536], replicated, may hold values from 0.5 to 1.5
- kernel: float32 [31, 1536], replicated, may hold values from -1 to 1
- bn_scale: float32 [1536], replicated, may hold values from 0.5 to 2
- bn_shift: float32 [1536], replicated, may hold values from -1 to 1
- ffn_gain: float32 [1536], replicated, may hold values from 0.5 to 1.5
- expert_ids: int32 [16, 4096, 2], P('fsdp', 'expert'), may hold values from 0 to 31, all different within a row; in each aligned block of 128 rows (0 to 127, 128 to 255, ..., all dimensions but the last counted through in order) at most 16 rows name the same one
- gates: float32 [16, 4096, 2], P('fsdp', 'expert'), may hold values from 0.1 to 1
- w_in: bfloat16 [32, 1536, 1536], P('expert', 'fsdp'), may hold values from -0.15625 to 0.15625
- w_out: bfloat16 [32, 1536, 1536], P('expert', 'fsdp'), may hold values from -0.15625 to 0.15625
Outputs:
- layer_out: bfloat16 [16, 4096, 1536], P('fsdp', 'expert')
Inputs may be any that keep to these rules, and one draw needn't show every extreme that they name: `expert_ids`: the 2 experts of a frame differ; within the 128 frames of one device (aligned blocks along a sequence) no expert is named more than 16 times, a bound that some block reaches.
All inputs are finite; a program needn't handle non-finite values.
Results may differ from a plain program's by a relative error of at most 0.0039.
Values may be sent and summed in bfloat16 or wider, within the bound.
No kernel may reach another device: no remote copies, remote signals or barrier semaphores. Data moves between devices by JAX's collectives and lax.ppermute only.
A program may use at most 64 MiB of HBM per device.

v0:
```python
import jax
import jax.numpy as jnp
from jax import lax
from jax.sharding import PartitionSpec as P

eps_norm = 1e-05


def padded_2(block, sides, width):
    for axis, dim in sides:
        count = lax.axis_size(axis)
        forward = [(i, i + 1) for i in range(count - 1)]
        backward = [(target, source) for source, target in forward]
        low = lax.ppermute(
            lax.slice_in_dim(block, block.shape[dim] - width, None, axis=dim), axis, forward
        )
        high = lax.ppermute(lax.slice_in_dim(block, 0, width, axis=dim), axis, backward)
        block = jnp.concatenate([low, block, high], axis=dim)
    return block


def layer_norm(values, gain):
    centre = jnp.mean(values, axis=-1, keepdims=True)
    centred = values - centre
    spread = jnp.mean(centred * centred, axis=-1, keepdims=True)
    return centred * lax.rsqrt(spread + eps_norm) * gain


def shards(frames, ln_gain, kernel, bn_scale, bn_shift, ffn_gain, expert_ids, gates, w_in, w_out):
    frame_count = frames.shape[1]
    width = frames.shape[2]
    taps = kernel.shape[0]
    reach = (taps - 1) // 2
    picks_per = expert_ids.shape[2]
    experts_all = lax.axis_size("expert") * w_in.shape[0]
    capacity = 2 * picks_per * frame_count // experts_all
    slots_all = experts_all * capacity
    stream = frames[0].astype(jnp.float32)
    normed = layer_norm(stream, ln_gain).astype(jnp.bfloat16)
    padded = padded_2(normed, (("expert", 0),), reach)
    filtered = jnp.zeros(stream.shape, jnp.float32)
    for offset in range(taps):
        filtered = filtered + kernel[offset] * padded[offset : offset + frame_count]
    mixed = stream + jax.nn.silu(bn_scale * filtered + bn_shift)
    routed = layer_norm(mixed, ffn_gain).astype(jnp.bfloat16)
    chosen = expert_ids[0].reshape(-1)
    onehot = (chosen[:, None] == jnp.arange(experts_all, dtype=jnp.int32)[None, :]).astype(
        jnp.int32
    )
    before = jnp.cumsum(onehot, axis=0) - onehot
    slot_at = jnp.sum(before * onehot, axis=1)
    target = (chosen * capacity + slot_at).reshape(frame_count, picks_per)
    placing = jnp.any(
        target[None, :, :] == jnp.arange(slots_all, dtype=jnp.int32)[:, None, None], axis=2
    )
    outgoing = jnp.dot(placing.astype(jnp.bfloat16), routed, preferred_element_type=jnp.float32)
    outgoing = outgoing.astype(jnp.bfloat16).reshape(experts_all, capacity, width)
    full_in, full_out = (
        lax.all_gather(w_in, "fsdp", axis=1, tiled=True),
        lax.all_gather(w_out, "fsdp", axis=1, tiled=True),
    )
    block = lax.all_to_all(outgoing, "expert", split_axis=0, concat_axis=0, tiled=True)
    rows_in = block.reshape(-1, width)
    hidden = jax.nn.silu(jnp.dot(rows_in, full_in[0], preferred_element_type=jnp.float32)).astype(
        jnp.bfloat16
    )
    result = jnp.dot(hidden, full_out[0], preferred_element_type=jnp.float32).astype(jnp.bfloat16)
    returned = lax.all_to_all(
        result.reshape(block.shape), "expert", split_axis=0, concat_axis=0, tiled=True
    )
    rows_back = returned.reshape(-1, width)
    picked = (
        jnp.take(rows_back, target.reshape(-1), axis=0)
        .reshape(frame_count, picks_per, width)
        .astype(jnp.float32)
    )
    combined = jnp.sum(gates[0][:, :, None] * picked, axis=1)
    return (mixed + 0.5 * combined).astype(jnp.bfloat16)[None]


def solution(mesh):
    return jax.shard_map(
        shards,
        mesh=mesh,
        in_specs=(
            P("fsdp", "expert", None),
            P(),
            P(),
            P(),
            P(),
            P(),
            P("fsdp", "expert", None),
            P("fsdp", "expert", None),
            P("expert", "fsdp", None),
            P("expert", "fsdp", None),
        ),
        out_specs=P("fsdp", "expert", None),
        check_vma=False,
    )
```

profile of v0, /device:TPU:8, one launch (start us, length us, event | category | flops | bytes accessed | tf_op | source)
XLA Modules:
  0.0 176.9 jit_solution(17045224739113966874)
XLA Ops:
  6.6 0.7 all-gather.3.cloned.1.call-update
  7.3 0.7 all-gather.5.cloned.1.call-update
  8.0 1.1 convert_reduce_fusion
  9.2 1.2 fusion.15
  10.4 1.3 fusion.17
  11.7 4.3 %collective-permute-start = (bf16[15,1536]{1,0:T(8,128)(2,1)S(1)}, bf16[15,1536]{1,0:T(8,128)(2,1)S(1)}, u32[]{:S(2)}, u32[]{:S(2)}) collective-permute-start(bf16[15,1536]{1,0:T(8,128)(2,1)S(1)} %get-tuple-element.38), channel_id=1, source_target_pairs={{0,1},{1,2},{2,3},{3,4},{4,5},{5,6},{6,7},{7,8},{8,9},{9,10},{10,1... | collective-permute-start | bytes 138248 | tf_op jit(solution)/shard_map/ppermute | solution.py:14
  16.0 1.3 collective-permute-start.1
  17.3 0.8 copy.26
  18.4 0.6 reduce-window.6
  19.0 0.2 slice_reduce_fusion
  19.5 1.4 slice_reduce_fusion.30
  21.0 1.9 %slice_reduce_fusion.31 = (f32[1536]{0:T(1024)S(1)}, f32[1536]{0:T(1024)S(1)}, f32[1536]{0:T(1024)S(1)}, f32[1536]{0:T(1024)S(1)}, f32[1536]{0:T(1024)S(1)}, /*i...) fusion(f32[31,1536]{1,0:T(8,128)} %param.12), kind=kLoop, calls=%fused_computation.145 | loop fusion | bytes 233472 | tf_op jit(solution)/shard_map/slice | solution.py:43
  23.0 4.3 %fusion.56 = (f32[128]{0:T(128)S(1)}, f32[128,1536]{1,0:T(8,128)S(1)}) fusion(f32[1536]{0:T(1024)S(1)} %copy-done.2, bf16[15,1536]{1,0:T(8,128)(2,1)S(1)} %collective-permute-done.1, bf16[128,1536]{1,0:T(8,128)(2,1)S(1)} %fusion.17, f32[1536]{0:T(1024)S(1)} %get-tuple-element.34, f32[1536]{0:T(1024)S(1)} %get-tuple-element.35, ...), kind=kLoop, calls=%fused_computation.158 | loop fusion | flops 37552000 | bytes 1868288 | tf_op jit(solution)/shard_map/reduce_sum | solution.py:23
  27.4 0.2 multiply_reduce_fusion.1
  27.6 0.7 convolution_convert_fusion
  28.3 54.0 %all_to_all.10 = bf16[32,16,1536]{2,1,0:T(8,128)(2,1)S(1)} all-to-all(bf16[32,16,1536]{2,1,0:T(8,128)(2,1)S(1)} %bitcast.66), channel_id=1, replica_groups=mesh['fsdp'=16,'expert'=32] {'expert'}, dimensions={0} | all-to-all | bytes 3145728 | tf_op jit(solution)/shard_map/all_to_all | solution.py:62
  82.2 21.9 %all-gather.5.cloned.1.call-done = bf16[1,1536,1536]{2,1,0:T(8,128)(2,1)} async-done(((bf16[1,96,1536]{2,1,0:T(8,128)(2,1)}), bf16[1,1536,1536]{2,1,0:T(8,128)(2,1)}) %all-gather.5.cloned.1.call-update) | async-done | bytes 4718608 | tf_op jit(solution)/shard_map/all_gather | solution.py:60
  104.1 10.3 %fusion.4 = bf16[512,1536]{1,0:T(8,128)(2,1)} fusion(bf16[1,1536,1536]{2,1,0:T(8,128)(2,1)} %all-gather.5.cloned.1.call-done, bf16[512,1536]{1,0:T(8,128)(2,1)S(1)} %bitcast.68, bf16[1,1536,1536]{2,1,0:T(8,128)(2,1)} %all-gather.3.cloned.1.call-done), kind=kOutput, calls=%fused_computation.6 | convolution fusion | flops 4836556800 | bytes 12582912 | tf_op jit(solution)/shard_map/dot_general | solution.py:67
  114.4 10.5 %all-to-all-start.1 = ((bf16[32,16,1536]{2,1,0:T(8,128)(2,1)}), bf16[32,16,1536]{2,1,0:T(8,128)(2,1)S(1)}, u32[]{:S(2)}, u32[]{:S(2)}) async-start(bf16[32,16,1536]{2,1,0:T(8,128)(2,1)} %bitcast.67), calls=%async_computation.1 | async-start | bytes 3145728 | tf_op jit(solution)/shard_map/all_to_all | solution.py:68
  125.7 38.9 %all-to-all-done.1 = bf16[32,16,1536]{2,1,0:T(8,128)(2,1)S(1)} async-done(((bf16[32,16,1536]{2,1,0:T(8,128)(2,1)}), bf16[32,16,1536]{2,1,0:T(8,128)(2,1)S(1)}, u32[]{:S(2)}, u32[]{:S(2)}) %all-to-all-start.1) | async-done | bytes 1572896 | tf_op jit(solution)/shard_map/all_to_all | solution.py:68
  164.5 1.3 gather_fusion
  165.8 0.3 gather.7
  166.1 3.1 %multiply_reduce_fusion = f32[128,1536]{1,0:T(8,128)S(1)} fusion(bf16[128,2,1536]{2,1,0:T(2,128)(2,1)S(1)} %gather.7, pred[128,2]{1,0:T(8,128)(4,1)S(1)} %copy.30, f32[128,2]{1,0:T(8,128)S(1)} %copy.25), kind=kLoop, calls=%fused_computation.36 | loop fusion | flops 1376256 | bytes 1574144 | tf_op jit(solution)/shard_map/reduce_sum | solution.py:77
  169.2 0.8 fusion.19
  (41 shorter events, 1.6 us)
Async XLA Ops:
  6.5 16.4 %copy-start = (bf16[1,128,1536]{2,1,0:T(8,128)(2,1)S(1)}, bf16[1,128,1536]{2,1,0:T(8,128)(2,1)}, u32[]{:S(2)}) copy-start(bf16[1,128,1536]{2,1,0:T(8,128)(2,1)} %param.10) | copy-start | bytes 1179652
  6.5 16.3 %copy-start.1 = (s32[1,128,2]{1,2,0:T(2,128)S(1)}, s32[1,128,2]{1,2,0:T(2,128)}, u32[]{:S(2)}) copy-start(s32[1,128,2]{1,2,0:T(2,128)} %param.16) | copy-start | bytes 3076
  6.5 16.4 %copy-start.3 = (f32[1536]{0:T(1024)S(1)}, f32[1536]{0:T(1024)}, u32[]{:S(2)}) copy-start(f32[1536]{0:T(1024)} %param.13) | copy-start | bytes 18436
  6.5 16.4 %copy-start.2 = (f32[1536]{0:T(1024)S(1)}, f32[1536]{0:T(1024)}, u32[]{:S(2)}) copy-start(f32[1536]{0:T(1024)} %param.14) | copy-start | bytes 18436
  6.5 21.0 %copy-start.4 = (f32[1536]{0:T(1024)S(1)}, f32[1536]{0:T(1024)}, u32[]{:S(2)}) copy-start(f32[1536]{0:T(1024)} %param.15) | copy-start | bytes 18436
  6.5 75.7 %all-gather.3.cloned.1.call-start = ((), (), s32[]{:S(2)}) async-start(), calls=%async_computation.2 | async-start | bytes 5013504 | tf_op jit(solution)/shard_map/all_gather | solution.py:59
  7.3 96.8 %all-gather.5.cloned.1.call-start = ((), (), s32[]{:S(2)}) async-start(), calls=%async_computation.3 | async-start | bytes 5013504 | tf_op jit(solution)/shard_map/all_gather | solution.py:60
  11.7 11.2 %collective-permute-start = (bf16[15,1536]{1,0:T(8,128)(2,1)S(1)}, bf16[15,1536]{1,0:T(8,128)(2,1)S(1)}, u32[]{:S(2)}, u32[]{:S(2)}) collective-permute-start(bf16[15,1536]{1,0:T(8,128)(2,1)S(1)} %get-tuple-element.38), channel_id=1, source_target_pairs={{0,1},{1,2},{2,3},{3,4},{4,5},{5,6},{6,7},{7,8},{8,9},{9,10},{10,1... | collective-permute-start | bytes 138248 | tf_op jit(solution)/shard_map/ppermute | solution.py:14
  16.0 6.9 %collective-permute-start.1 = (bf16[15,1536]{1,0:T(8,128)(2,1)S(1)}, bf16[15,1536]{1,0:T(8,128)(2,1)S(1)}, u32[]{:S(2)}, u32[]{:S(2)}) collective-permute-start(bf16[15,1536]{1,0:T(8,128)(2,1)S(1)} %get-tuple-element.39), channel_id=1, source_target_pairs={{1,0},{2,1},{3,2},{4,3},{5,4},{6,5},{7,6},{8,7},{9,8},{10,9},{11,1... | collective-permute-start | bytes 138248 | tf_op jit(solution)/shard_map/ppermute | solution.py:17
  114.4 11.1 %copy-start.5 = (f32[1,128,2]{1,2,0:T(2,128)S(1)}, f32[1,128,2]{1,2,0:T(2,128)}, u32[]{:S(2)}) copy-start(f32[1,128,2]{1,2,0:T(2,128)} %param.17) | copy-start | bytes 3076
  114.4 50.1 %all-to-all-start.1 = ((bf16[32,16,1536]{2,1,0:T(8,128)(2,1)}), bf16[32,16,1536]{2,1,0:T(8,128)(2,1)S(1)}, u32[]{:S(2)}, u32[]{:S(2)}) async-start(bf16[32,16,1536]{2,1,0:T(8,128)(2,1)} %bitcast.67), calls=%async_computation.1 | async-start | bytes 3145728 | tf_op jit(solution)/shard_map/all_to_all | solution.py:68
Sparse Core Ops, SparseCore 0:
  9.5 48.9 all-gather.2
  60.5 43.5 all-gather.4
where the time goes:
time: 177 us
  waiting for transfers between devices  62.1 us (35%)
  blocking collectives  54 us (31%)
  starting transfers between devices  16.1 us (9%)
  between operations  13.6 us (8%)
  other arithmetic  13 us (7%)
  matrix products  10.9 us (6%)
  local copies, waits for them, and re-layouts  7.04 us (4%)
    all_to_all x1, blocking collectives, shards(): lax.all_to_all(outgoing, 'expert', split_axis=0, concat_axis=0, tiled=True)  54 us
    all_to_all x1, waiting for transfers between devices, shards(): lax.all_to_all(result.reshape(block.shape), 'expert', split_axis=0, conca...  38.9 us
    all_gather x1, waiting for transfers between devices, shards(): lax.all_gather(w_out, 'fsdp', axis=1, tiled=True)  21.9 us
    all_to_all x1, starting transfers between devices, shards(): lax.all_to_all(result.reshape(block.shape), 'expert', split_axis=0, conca...  10.5 us
    dot_general x1, matrix products, shards(): jnp.dot(hidden, full_out[0], preferred_element_type=jnp.float32)  10.3 us
    reduce_sum x2, other arithmetic, layer_norm(): centre = jnp.mean(values, axis=-1, keepdims=True)  5.48 us
    ppermute x1, starting transfers between devices, padded_2(): lax.ppermute(lax.slice_in_dim(block, block.shape[dim] - width, None, axis...  4.28 us
  transfers between devices with their start and end apart: 5, of which 2 were waited for; matrix products, arithmetic and copies ran while one was open for 9% of the time, Pallas kernels for 0%

commit v1 on v0

--- a/solution.py
+++ b/solution.py
@@ -57,7 +57,9 @@
     outgoing = outgoing.astype(jnp.bfloat16).reshape(experts_all, capacity, width)
     full_in, full_out = (
         lax.all_gather(w_in, "fsdp", axis=1, tiled=True),
-        lax.all_gather(w_out, "fsdp", axis=1, tiled=True),
+        jnp.concatenate(
+            lax.all_to_all(jnp.stack([w_out] * lax.axis_size("fsdp")), "fsdp", 0, 0), axis=1
+        ),
     )
     block = lax.all_to_all(outgoing, "expert", split_axis=0, concat_axis=0, tiled=True)
     rows_in = block.reshape(-1, width)

time: 177 us -> 287 us (1.62)
  the two profiles are of different devices: /device:TPU:8 before, /device:TPU:24 now
where the time goes in v1:
time: 287 us
  waiting for transfers between devices  166 us (58%)
  blocking collectives  54 us (19%)
  starting transfers between devices  17.9 us (6%)
  other arithmetic  14.6 us (5%)
  between operations  13.6 us (5%)
  matrix products  10.9 us (4%)
  local copies, waits for them, and re-layouts  9.89 us (3%)
    all_to_all x1, waiting for transfers between devices, shards(): lax.all_to_all(jnp.stack([w_out] * lax.axis_size('fsdp')), 'fsdp', 0, 0)  126 us
    all_to_all x1, blocking collectives, shards(): lax.all_to_all(outgoing, 'expert', split_axis=0, concat_axis=0, tiled=True)  54 us
    all_to_all x1, waiting for transfers between devices, shards(): lax.all_to_all(result.reshape(block.shape), 'expert', split_axis=0, conca...  38.8 us
    dot_general x1, matrix products, shards(): jnp.dot(hidden, full_out[0], preferred_element_type=jnp.float32)  10.3 us
    all_to_all x1, starting transfers between devices, shards(): lax.all_to_all(jnp.stack([w_out] * lax.axis_size('fsdp')), 'fsdp', 0, 0)  7.35 us
    reduce_sum x2, other arithmetic, layer_norm(): centre = jnp.mean(values, axis=-1, keepdims=True)  6.34 us
  transfers between devices with their start and end apart: 5, of which 2 were waited for; matrix products, arithmetic and copies ran while one was open for 2% of the time, Pallas kernels for 0%

profile of v1, /device:TPU:24, one launch (start us, length us, event | category | flops | bytes accessed | tf_op | source)
XLA Modules:
  0.0 286.8 jit_solution(11505619480484774241)
XLA Ops:
  6.5 1.2 convert_reduce_fusion
  7.7 1.2 fusion.10
  9.0 1.3 fusion.12
  10.3 4.3 %collective-permute-start = (bf16[15,1536]{1,0:T(8,128)(2,1)S(1)}, bf16[15,1536]{1,0:T(8,128)(2,1)S(1)}, u32[]{:S(2)}, u32[]{:S(2)}) collective-permute-start(bf16[15,1536]{1,0:T(8,128)(2,1)S(1)} %get-tuple-element.38), channel_id=1, source_target_pairs={{0,1},{1,2},{2,3},{3,4},{4,5},{5,6},{6,7},{7,8},{8,9},{9,10},{10,1... | collective-permute-start | bytes 138248 | tf_op jit(solution)/shard_map/ppermute | solution.py:14
  14.6 1.3 collective-permute-start.1
  15.9 1.9 slice_reduce_fusion.31
  17.8 1.5 slice_reduce_fusion.30
  19.4 0.8 copy.26
  20.4 0.6 reduce-window.6
  21.6 0.7 broadcast_multiply_fusion
  22.4 5.1 %fusion.51 = (f32[128]{0:T(128)S(1)}, f32[128,1536]{1,0:T(8,128)S(1)}) fusion(f32[1536]{0:T(1024)} %param.14, bf16[15,1536]{1,0:T(8,128)(2,1)S(1)} %collective-permute-done.1, bf16[128,1536]{1,0:T(8,128)(2,1)S(1)} %fusion.12, f32[1536]{0:T(1024)S(1)} %get-tuple-element.34, f32[1536]{0:T(1024)S(1)} %get-tuple-element.35, f32[1536]{0:T(1024)S(1)} %get-tuple-element.6, ...), kind=kLoop, calls=%fused_computation.156 | loop fusion | flops 37552000 | bytes 1868288 | tf_op jit(solution)/shard_map/reduce_sum | solution.py:23
  27.8 0.7 convolution_convert_fusion.1
  28.5 54.0 %all_to_all.15 = bf16[32,16,1536]{2,1,0:T(8,128)(2,1)S(1)} all-to-all(bf16[32,16,1536]{2,1,0:T(8,128)(2,1)S(1)} %bitcast.64), channel_id=1, replica_groups=mesh['fsdp'=16,'expert'=32] {'expert'}, dimensions={0} | all-to-all | bytes 3145728 | tf_op jit(solution)/shard_map/all_to_all | solution.py:64
  82.4 2.7 stack.2
  85.1 7.4 %all-to-all-start.1 = ((bf16[16,1,96,1536]{3,2,1,0:T(8,128)(2,1)}), bf16[16,1,96,1536]{3,2,1,0:T(8,128)(2,1)}, u32[]{:S(2)}, u32[]{:S(2)}) async-start(bf16[16,1,96,1536]{3,2,1,0:T(8,128)(2,1)} %stack.2), calls=%async_computation.1 | async-start | bytes 9437184 | tf_op jit(solution)/shard_map/all_to_all | solution.py:61
  92.5 0.7 all-gather.2.cloned.1.call-update
  93.2 126.3 %all-to-all-done.1 = bf16[16,1,96,1536]{3,2,1,0:T(8,128)(2,1)} async-done(((bf16[16,1,96,1536]{3,2,1,0:T(8,128)(2,1)}), bf16[16,1,96,1536]{3,2,1,0:T(8,128)(2,1)}, u32[]{:S(2)}, u32[]{:S(2)}) %all-to-all-start.1) | async-done | bytes 4718624 | tf_op jit(solution)/shard_map/all_to_all | solution.py:61
  219.6 10.3 %convolution_convert_fusion = bf16[512,1536]{1,0:T(8,128)(2,1)} fusion(bf16[1536,1536]{1,0:T(8,128)(2,1)} %bitcast.9, bf16[512,1536]{1,0:T(8,128)(2,1)S(1)} %bitcast.66, bf16[1,1536,1536]{2,1,0:T(8,128)(2,1)} %all-gather.2.cloned.1.call-done), kind=kOutput, calls=%fused_computation.4 | convolution fusion | flops 4836556800 | bytes 12582912 | tf_op jit(solution)/shard_map/dot_general | solution.py:69
  229.8 5.0 %all-to-all-start.2 = ((bf16[32,16,1536]{2,1,0:T(8,128)(2,1)}), bf16[32,16,1536]{2,1,0:T(8,128)(2,1)S(1)}, u32[]{:S(2)}, u32[]{:S(2)}) async-start(bf16[32,16,1536]{2,1,0:T(8,128)(2,1)} %bitcast.65), calls=%async_computation.2 | async-start | bytes 3145728 | tf_op jit(solution)/shard_map/all_to_all | solution.py:70
  235.6 38.8 %all-to-all-done.2 = bf16[32,16,1536]{2,1,0:T(8,128)(2,1)S(1)} async-done(((bf16[32,16,1536]{2,1,0:T(8,128)(2,1)}), bf16[32,16,1536]{2,1,0:T(8,128)(2,1)S(1)}, u32[]{:S(2)}, u32[]{:S(2)}) %all-to-all-start.2) | async-done | bytes 1572896 | tf_op jit(solution)/shard_map/all_to_all | solution.py:70
  274.4 1.3 gather_fusion
  275.7 0.3 gather.7
  276.0 3.1 %multiply_reduce_fusion = f32[128,1536]{1,0:T(8,128)S(1)} fusion(bf16[128,2,1536]{2,1,0:T(2,128)(2,1)S(1)} %gather.7, pred[128,2]{1,0:T(8,128)(4,1)S(1)} %copy.30, f32[128,2]{1,0:T(8,128)S(1)} %copy.25), kind=kLoop, calls=%fused_computation.34 | loop fusion | flops 1376256 | bytes 1574144 | tf_op jit(solution)/shard_map/reduce_sum | solution.py:79
  279.1 0.8 fusion.14
  (39 shorter events, 1.9 us)
Async XLA Ops:
  6.5 15.8 %copy-start = (bf16[1,128,1536]{2,1,0:T(8,128)(2,1)S(1)}, bf16[1,128,1536]{2,1,0:T(8,128)(2,1)}, u32[]{:S(2)}) copy-start(bf16[1,128,1536]{2,1,0:T(8,128)(2,1)} %param.10) | copy-start | bytes 1179652
  6.5 21.3 %copy-start.3 = (f32[1536]{0:T(1024)S(1)}, f32[1536]{0:T(1024)}, u32[]{:S(2)}) copy-start(f32[1536]{0:T(1024)} %param.15) | copy-start | bytes 18436
  10.3 12.0 %collective-permute-start = (bf16[15,1536]{1,0:T(8,128)(2,1)S(1)}, bf16[15,1536]{1,0:T(8,128)(2,1)S(1)}, u32[]{:S(2)}, u32[]{:S(2)}) collective-permute-start(bf16[15,1536]{1,0:T(8,128)(2,1)S(1)} %get-tuple-element.38), channel_id=1, source_target_pairs={{0,1},{1,2},{2,3},{3,4},{4,5},{5,6},{6,7},{7,8},{8,9},{9,10},{10,1... | collective-permute-start | bytes 138248 | tf_op jit(solution)/shard_map/ppermute | solution.py:14
  14.6 7.8 %collective-permute-start.1 = (bf16[15,1536]{1,0:T(8,128)(2,1)S(1)}, bf16[15,1536]{1,0:T(8,128)(2,1)S(1)}, u32[]{:S(2)}, u32[]{:S(2)}) collective-permute-start(bf16[15,1536]{1,0:T(8,128)(2,1)S(1)} %get-tuple-element.39), channel_id=1, source_target_pairs={{1,0},{2,1},{3,2},{4,3},{5,4},{6,5},{7,6},{8,7},{9,8},{10,9},{11,1... | collective-permute-start | bytes 138248 | tf_op jit(solution)/shard_map/ppermute | solution.py:17
  27.5 54.9 %copy-start.1 = (bf16[1,96,1536]{2,1,0:T(8,128)(2,1)S(1)}, bf16[1,96,1536]{2,1,0:T(8,128)(2,1)}, u32[]{:S(2)}) copy-start(bf16[1,96,1536]{2,1,0:T(8,128)(2,1)} %param.19) | copy-start | bytes 884740
  85.1 134.4 %all-to-all-start.1 = ((bf16[16,1,96,1536]{3,2,1,0:T(8,128)(2,1)}), bf16[16,1,96,1536]{3,2,1,0:T(8,128)(2,1)}, u32[]{:S(2)}, u32[]{:S(2)}) async-start(bf16[16,1,96,1536]{3,2,1,0:T(8,128)(2,1)} %stack.2), calls=%async_computation.1 | async-start | bytes 9437184 | tf_op jit(solution)/shard_map/all_to_all | solution.py:61
  92.5 127.1 %all-gather.2.cloned.1.call-start = ((), (), s32[]{:S(2)}) async-start(), calls=%async_computation.3 | async-start | bytes 5013504 | tf_op jit(solution)/shard_map/all_gather | solution.py:59
  229.8 5.4 %copy-start.2 = (s32[1,128,2]{1,2,0:T(2,128)S(1)}, s32[1,128,2]{1,2,0:T(2,128)}, u32[]{:S(2)}) copy-start(s32[1,128,2]{1,2,0:T(2,128)} %param.16) | copy-start | bytes 3076
  229.8 5.6 %copy-start.4 = (f32[1,128,2]{1,2,0:T(2,128)S(1)}, f32[1,128,2]{1,2,0:T(2,128)}, u32[]{:S(2)}) copy-start(f32[1,128,2]{1,2,0:T(2,128)} %param.17) | copy-start | bytes 3076
  229.8 44.6 %all-to-all-start.2 = ((bf16[32,16,1536]{2,1,0:T(8,128)(2,1)}), bf16[32,16,1536]{2,1,0:T(8,128)(2,1)S(1)}, u32[]{:S(2)}, u32[]{:S(2)}) async-start(bf16[32,16,1536]{2,1,0:T(8,128)(2,1)} %bitcast.65), calls=%async_computation.2 | async-start | bytes 3145728 | tf_op jit(solution)/shard_map/all_to_all | solution.py:70
Sparse Core Ops, SparseCore 0:
  95.4 106.4 all-gather.1
